TPU v7x, 512 devices: a whole 4x4x16 slice. The times are simulated.
512 devices in a mesh: dp: 32 (over y_hi, z), tensor: 16 (over x, y_lo, core).
Axes of the slice: x: 4, y: 4 (y_hi: 2, y_lo: 2; y = y_hi * 2 + y_lo), z: 16, core: 2. Of those that a mesh axis runs over, the one named last changes fastest.
Arguments:
- residual: bfloat16 [65536, 2048], P(('dp', 'tensor')), may hold values from -0.59765625 to 0.59765625
- queries: bfloat16 [65536, 2048], P(('dp', 'tensor')), may hold values from -27 to 27
- new_keys: bfloat16 [65536, 2048], P(('dp', 'tensor')), may hold values from -27 to 27
- new_values: bfloat16 [65536, 2048], P(('dp', 'tensor')), may hold values from -6 to 6
- lengths: int32 [32, 2], P('dp'), may hold values from 1 to 1536, 2048 in all within a row
- page_order: int32 [32, 17], P('dp'), may hold values from 0 to 16, each once within a row
- wo_shard: float32 [2048, 2048], P('tensor', 'dp'), may hold values from -0.125 to 0.125
- norm_gain: float32 [2048], replicated, may hold values from 0.1 to 1.9
- gate_shard: float32 [16, 2048, 256], P('tensor', 'dp'), may hold values from -0.125 to 0.125
- up_shard: float32 [16, 2048, 256], P('tensor', 'dp'), may hold values from -0.125 to 0.125
- down_shard: float32 [16, 256, 2048], P('tensor', None, 'dp'), may hold values from -0.1875 to 0.1875
- routes: int32 [65536, 8], P(('dp', 'tensor')), may hold values from 0 to 63, as said below
- route_weights: float32 [65536, 8], P(('dp', 'tensor')), may hold values from 0.05 to 0.3
Outputs:
- hidden_mid: bfloat16 [65536, 2048], P(('dp', 'tensor'))
- expert_sum: bfloat16 [65536, 2048], P(('dp', 'tensor'))
- key_pages: bfloat16 [544, 128, 2048], P('dp', None, 'tensor')
- value_pages: bfloat16 [544, 128, 2048], P('dp', None, 'tensor')
Inputs may be any that keep to these rules, and one draw needn't show every extreme that they name: `routes`: each row names 8 different experts. Within each aligned block of 128 rows (the rows of one device), each expert below 4 is named by 1 to 16 rows; one of them, the same in all blocks of a draw, by exactly 16 rows in every block, the others by at most 8 rows.
All inputs are finite; a program needn't handle non-finite values.
Results may differ from a plain program's by a relative error of at most 0.015.
Values may be sent and summed in bfloat16 or wider, within the bound.
No kernel may reach another device: no remote copies, remote signals or barrier semaphores. Data moves between devices by JAX's collectives and lax.ppermute only.
A program may use at most 64 MiB of HBM per device.

v0:
```python
import math
import jax
import jax.numpy as jnp
from jax import lax
from jax.sharding import PartitionSpec as P

D = 2048
HEADS = 16
HD = 128
SPLIT = 4
PAGE = 128
MOST = 16


def page_layout(lens_row, order_row, group_rows, pool_size):
    index_rows = jnp.arange(group_rows, dtype=jnp.int32)
    prompt_ends = jnp.cumsum(lens_row)
    segment = jnp.sum((index_rows[:, None] >= prompt_ends[None, :]).astype(jnp.int32), axis=1)
    prompt_starts = prompt_ends - lens_row
    owner_mask = (
        segment[:, None] == jnp.arange(lens_row.shape[0], dtype=jnp.int32)[None, :]
    ).astype(jnp.int32)
    begins = jnp.sum(owner_mask * prompt_starts[None, :], axis=1)
    page_count = (lens_row + PAGE - 1) // PAGE
    first_page = jnp.cumsum(page_count) - page_count
    page_first = jnp.sum(owner_mask * first_page[None, :], axis=1)
    position = index_rows - begins
    logical = page_first + position // PAGE
    matched = (logical[:, None] == jnp.arange(pool_size, dtype=jnp.int32)[None, :]).astype(
        jnp.int32
    )
    physical = jnp.sum(matched * order_row[None, :], axis=1)
    return (segment, physical * PAGE + position % PAGE)


def attend_group(q_heads, k_heads, v_heads, segment, heads_here):
    group_rows = q_heads.shape[0]
    block_rows = min(512, group_rows)
    count_blocks = group_rows // block_rows
    q_blocks = q_heads.reshape(count_blocks, block_rows, heads_here, HD)
    seg_blocks = segment.reshape(count_blocks, block_rows)
    k_split = k_heads.reshape(group_rows, heads_here, HD)
    v_split = v_heads.reshape(group_rows, heads_here, HD)

    def one_block(block_pair):
        q_block, seg_block = block_pair
        scores = jnp.einsum(
            "qhd,khd->hqk", q_block, k_split, preferred_element_type=jnp.float32
        ) / math.sqrt(HD)
        same_prompt = seg_block[:, None] == segment[None, :]
        scores = jnp.where(same_prompt[None, :, :], scores, -jnp.inf)
        row_max = jnp.max(scores, axis=2, keepdims=True)
        weights = jnp.exp(scores - row_max)
        totals = jnp.sum(weights, axis=2)
        output = jnp.einsum(
            "hqk,khd->qhd",
            weights.astype(jnp.bfloat16),
            v_split,
            preferred_element_type=jnp.float32,
        )
        output = output / jnp.transpose(totals)[:, :, None]
        return output.astype(jnp.bfloat16).reshape(block_rows, heads_here * HD)

    return lax.map(one_block, (q_blocks, seg_blocks)).reshape(group_rows, heads_here * HD)


def body(
    residual,
    queries,
    new_keys,
    new_values,
    lengths,
    page_order,
    wo_shard,
    norm_gain,
    gate_shard,
    up_shard,
    down_shard,
    routes,
    route_weights,
):
    tensor_count = lax.axis_size("tensor")
    heads_here = HEADS // tensor_count
    q_heads, k_heads, v_heads = (
        lax.all_to_all(queries, "tensor", split_axis=1, concat_axis=0, tiled=True),
        lax.all_to_all(new_keys, "tensor", split_axis=1, concat_axis=0, tiled=True),
        lax.all_to_all(new_values, "tensor", split_axis=1, concat_axis=0, tiled=True),
    )
    group_rows = q_heads.shape[0]
    pool_size = page_order.shape[1]
    segment, slot_index = page_layout(lengths[0], page_order[0], group_rows, pool_size)
    head_width = k_heads.shape[1]
    key_pages = (
        jnp.zeros((pool_size * PAGE, head_width), jnp.bfloat16)
        .at[slot_index]
        .set(k_heads)
        .reshape(pool_size, PAGE, head_width)
    )
    value_pages = (
        jnp.zeros((pool_size * PAGE, head_width), jnp.bfloat16)
        .at[slot_index]
        .set(v_heads)
        .reshape(pool_size, PAGE, head_width)
    )
    attended = attend_group(q_heads, k_heads, v_heads, segment, heads_here)
    token_rows = lax.all_to_all(attended, "tensor", split_axis=0, concat_axis=1, tiled=True)
    wo_cast = wo_shard.astype(jnp.bfloat16)
    columns = lax.all_gather(wo_cast, "dp", axis=1, tiled=True)
    projected = jnp.dot(
        token_rows,
        lax.all_gather(columns, "tensor", axis=0, tiled=True),
        preferred_element_type=jnp.float32,
    )
    hidden_mid = (residual.astype(jnp.float32) + projected).astype(jnp.bfloat16)
    mid_float = hidden_mid.astype(jnp.float32)
    normed = (
        mid_float
        * lax.rsqrt(jnp.mean(mid_float * mid_float, axis=1, keepdims=True) + 1e-06)
        * norm_gain
    ).astype(jnp.bfloat16)
    flight = tensor_count // SPLIT
    flight_ids = jnp.arange(flight, dtype=jnp.int32)
    named_here = routes[:, :, None] == flight_ids[None, None, :]
    routed = jnp.any(named_here, axis=1)
    weight_sum = jnp.sum(jnp.where(named_here, route_weights[:, :, None], 0.0), axis=1)
    ranked = jnp.cumsum(routed.astype(jnp.int32), axis=0) - 1
    picked = (ranked[:, :, None] == jnp.arange(MOST, dtype=jnp.int32)[None, None, :]) & routed[
        :, :, None
    ]
    outgoing = jnp.einsum(
        "tem,td->emd", picked.astype(jnp.bfloat16), normed, preferred_element_type=jnp.float32
    ).astype(jnp.bfloat16)
    outgoing = jnp.repeat(outgoing, SPLIT, axis=0)
    gate_full, up_full, down_full = (
        lax.all_gather(gate_shard.astype(jnp.bfloat16), "dp", axis=1, tiled=True),
        lax.all_gather(up_shard.astype(jnp.bfloat16), "dp", axis=1, tiled=True),
        lax.all_gather(down_shard.astype(jnp.bfloat16), "dp", axis=2, tiled=True),
    )
    arrived = lax.all_to_all(outgoing, "tensor", split_axis=0, concat_axis=0, tiled=True)
    gate_val = jnp.einsum("smd,dp->smp", arrived, gate_full[0], preferred_element_type=jnp.float32)
    up_val = jnp.einsum("smd,dp->smp", arrived, up_full[0], preferred_element_type=jnp.float32)
    inner_act = (jax.nn.silu(gate_val) * up_val).astype(jnp.bfloat16)
    result = jnp.einsum(
        "smp,pd->smd", inner_act, down_full[0], preferred_element_type=jnp.float32
    ).astype(jnp.bfloat16)
    returned = lax.all_to_all(result, "tensor", split_axis=0, concat_axis=0, tiled=True)
    summed = jnp.sum(returned.reshape(flight, SPLIT, MOST, D).astype(jnp.float32), axis=1)
    mixing = picked.astype(jnp.float32) * weight_sum[:, :, None]
    expert_sum = jnp.einsum("tem,emd->td", mixing, summed, precision=lax.Precision.HIGHEST).astype(
        jnp.bfloat16
    )
    return (hidden_mid, expert_sum, key_pages, value_pages)


def solution(mesh):
    return jax.shard_map(
        body,
        mesh=mesh,
        in_specs=(
            P(("dp", "tensor"), None),
            P(("dp", "tensor"), None),
            P(("dp", "tensor"), None),
            P(("dp", "tensor"), None),
            P("dp", None),
            P("dp", None),
            P("tensor", "dp"),
            P(),
            P("tensor", "dp", None),
            P("tensor", "dp", None),
            P("tensor", None, "dp"),
            P(("dp", "tensor"), None),
            P(("dp", "tensor"), None),
        ),
        out_specs=(
            P(("dp", "tensor"), None),
            P(("dp", "tensor"), None),
            P("dp", None, "tensor"),
            P("dp", None, "tensor"),
        ),
        check_vma=False,
    )
```

profile of v0, /device:TPU:1, one launch (start us, length us, event | category | flops | bytes accessed | tf_op | source)
XLA Modules:
  0.0 635.9 jit_solution(6192346306838084614)
XLA Ops:
  8.1 77.1 %all_gather.15 = bf16[128,2048]{0,1:T(8,128)(2,1)} all-gather(bf16[128,64]{0,1:T(8,128)(2,1)S(1)} %convert_element_type.68), channel_id=1, replica_groups=mesh['dp'=32,'tensor'=16] {'dp'}, dimensions={1}, use_global_device_ids=true | all-gather | bytes 540672 | tf_op jit(solution)/shard_map/all_gather | solution.py:108
  85.2 1.4 convert_element_type.74
  86.7 2.0 copy.76
  88.7 19.2 %all-to-all-start.1 = ((bf16[128,16,128]{0,2,1:T(8,128)(2,1)}), bf16[128,16,128]{0,2,1:T(8,128)(2,1)S(1)}, u32[]{:S(2)}, u32[]{:S(2)}) async-start(bf16[128,16,128]{0,2,1:T(8,128)(2,1)} %bitcast.14), calls=%async_computation.1 | async-start | bytes 1048576 | tf_op jit(solution)/shard_map/all_to_all | solution.py:86
  107.9 2.0 copy.78
  109.9 9.6 %all-to-all-done.1 = bf16[128,16,128]{0,2,1:T(8,128)(2,1)S(1)} async-done(((bf16[128,16,128]{0,2,1:T(8,128)(2,1)}), bf16[128,16,128]{0,2,1:T(8,128)(2,1)S(1)}, u32[]{:S(2)}, u32[]{:S(2)}) %all-to-all-start.1) | async-done | bytes 524320 | tf_op jit(solution)/shard_map/all_to_all | solution.py:86
  119.5 4.6 all-to-all-start.2
  124.1 1.0 copy.74
  125.1 12.6 %all-to-all-done.2 = bf16[128,16,128]{0,2,1:T(8,128)(2,1)S(1)} async-done(((bf16[128,16,128]{0,2,1:T(8,128)(2,1)}), bf16[128,16,128]{0,2,1:T(8,128)(2,1)S(1)}, u32[]{:S(2)}, u32[]{:S(2)}) %all-to-all-start.2) | async-done | bytes 524320 | tf_op jit(solution)/shard_map/all_to_all | solution.py:87
  137.8 5.7 all-to-all-start
  145.1 11.8 %all-to-all-done = bf16[128,16,128]{0,2,1:T(8,128)(2,1)S(1)} async-done(((bf16[128,16,128]{0,2,1:T(8,128)(2,1)}), bf16[128,16,128]{0,2,1:T(8,128)(2,1)S(1)}, u32[]{:S(2)}, u32[]{:S(2)}) %all-to-all-start) | async-done | bytes 524320 | tf_op jit(solution)/shard_map/all_to_all | solution.py:85
  157.2 12.3 %while.10 = (s32[]{:T(128)}, bf16[4,512,128]{2,1,0:T(8,128)(2,1)}, s32[4,512]{1,0:T(4,128)S(1)}, s32[2048]{0:T(1024)S(1)}, bf16[4,512,1,128]{3,1,2,0:T(8,128)(2,...) while((s32[]{:T(128)}, bf16[4,512,128]{2,1,0:T(8,128)(2,1)}, ...), condition=%wide.region_5.6_spmd, body=%wide.region_2.0_spmd.sunk | while | flops 545389568 | bytes 13918813 | solution.py:64
  157.2 0.9 fusion.83
  158.8 1.5 fusion.85
  161.9 1.4 fusion.85
  165.0 1.5 fusion.85
  168.0 1.5 fusion.85
  169.5 4.9 all-to-all-start.3
  175.5 8.6 %all-to-all-done.3 = bf16[16,128,128]{2,1,0:T(8,128)(2,1)S(1)} async-done(((bf16[16,128,128]{2,1,0:T(8,128)(2,1)}), bf16[16,128,128]{2,1,0:T(8,128)(2,1)S(1)}, u32[]{:S(2)}, u32[]{:S(2)}) %all-to-all-start.3) | async-done | bytes 524320 | tf_op jit(solution)/shard_map/all_to_all | solution.py:106
  184.4 6.4 %fusion.28 = (f32[128]{0:T(128)S(1)}, bf16[128,2048]{1,0:T(8,128)(2,1)S(1)}) fusion(bf16[128,2048]{0,1:T(8,128)(2,1)S(1)} %bitcast.108, bf16[2048,2048]{0,1:T(8,128)(2,1)} %all-gather.5.cloned.1.call-done, bf16[128,2048]{1,0:T(8,128)(2,1)S(1)} %copy-done), kind=kOutput, calls=%fused_computation.30 | convolution fusion | flops 1075314560 | bytes 9961984 | tf_op jit(solution)/shard_map/dot_general | solution.py:109
  191.2 1.1 broadcast_in_dim.27
  192.3 4.7 all-to-all-start.4
  197.3 114.6 %all-gather.7.cloned.1.call-done = bf16[1,2048,256]{2,1,0:T(8,128)(2,1)} async-done(((bf16[1,64,256]{2,1,0:T(8,128)(2,1)}), bf16[1,2048,256]{2,1,0:T(8,128)(2,1)}) %all-gather.7.cloned.1.call-update) | async-done | bytes 1048592 | tf_op jit(solution)/shard_map/all_gather | solution.py:135
  311.9 1.7 fusion.34
  313.6 139.5 %all-gather.11.cloned.1.call-done = bf16[1,256,2048]{1,2,0:T(8,128)(2,1)} async-done(((bf16[1,256,64]{1,2,0:T(8,128)(2,1)}), bf16[1,256,2048]{1,2,0:T(8,128)(2,1)}) %all-gather.11.cloned.1.call-update) | async-done | bytes 1048592 | tf_op jit(solution)/shard_map/all_gather | solution.py:137
  453.0 141.0 %all-gather.9.cloned.1.call-done = bf16[1,2048,256]{2,1,0:T(8,128)(2,1)} async-done(((bf16[1,64,256]{2,1,0:T(8,128)(2,1)}), bf16[1,2048,256]{2,1,0:T(8,128)(2,1)}) %all-gather.9.cloned.1.call-update) | async-done | bytes 1048592 | tf_op jit(solution)/shard_map/all_gather | solution.py:136
  594.0 3.8 convolution_convert_fusion
  597.8 14.0 %all-to-all-start.5 = ((bf16[16,16,2048]{2,1,0:T(8,128)(2,1)}), bf16[16,16,2048]{2,1,0:T(8,128)(2,1)S(1)}, u32[]{:S(2)}, u32[]{:S(2)}) async-start(bf16[16,16,2048]{2,1,0:T(8,128)(2,1)} %convolution_convert_fusion), calls=%async_computation.5 | async-start | bytes 2097152 | tf_op jit(solution)/shard_map/all_to_all | solution.py:146
  612.1 6.5 %scatter_custom_fusion = bf16[2176,128]{1,0:T(8,128)(2,1)} fusion(s32[2048]{0:T(1024)S(1)} %bitcast.121, bf16[2048,128]{1,0:T(8,128)(2,1)S(1)} %bitcast.116, bf16[]{:T(256)} %constant.81.clone.1), kind=kCustom, calls=%fused_computation.42 | custom fusion | bytes 557058 | tf_op jit(solution)/shard_map/scatter | solution.py:96
  618.6 6.5 %scatter_custom_fusion.1 = bf16[2176,128]{1,0:T(8,128)(2,1)} fusion(s32[2048]{0:T(1024)S(1)} %bitcast.122, bf16[2048,128]{1,0:T(8,128)(2,1)S(1)} %bitcast.107, bf16[]{:T(256)} %constant.81.clone.1), kind=kCustom, calls=%fused_computation.40 | custom fusion | bytes 557058 | tf_op jit(solution)/shard_map/scatter | solution.py:102
  625.2 2.2 all-to-all-done.5
  627.5 1.8 fusion.26
  (70 shorter events, 10.7 us)
Async XLA Ops:
  7.2 116.9 %copy-start.2 = (bf16[128,2048]{1,0:T(8,128)(2,1)S(1)}, bf16[128,2048]{1,0:T(8,128)(2,1)}, u32[]{:S(2)}) copy-start(bf16[128,2048]{1,0:T(8,128)(2,1)} %param.16) | copy-start | bytes 1572868
  7.2 136.3 %copy-start.3 = (f32[1,256,64]{1,2,0:T(8,128)S(1)}, f32[1,256,64]{1,2,0:T(8,128)}, u32[]{:S(2)}) copy-start(f32[1,256,64]{1,2,0:T(8,128)} %param.25) | copy-start | bytes 196612
  7.2 137.0 %copy-start.8 = (s32[1,2]{1,0:T(1,128)S(1)}, s32[1,2]{1,0:T(1,128)}, u32[]{:S(2)}) copy-start(s32[1,2]{1,0:T(1,128)} %param.19) | copy-start | bytes 28
  7.2 177.2 %all-gather.5.cloned.1.call-start = ((), (), s32[]{:S(2)}) async-start(), calls=%async_computation.6 | async-start | bytes 8912896 | tf_op jit(solution)/shard_map/all_gather | solution.py:111
  85.2 226.8 %all-gather.7.cloned.1.call-start = ((), (), s32[]{:S(2)}) async-start(), calls=%async_computation.7 | async-start | bytes 1081344 | tf_op jit(solution)/shard_map/all_gather | solution.py:135
  88.7 30.8 %all-to-all-start.1 = ((bf16[128,16,128]{0,2,1:T(8,128)(2,1)}), bf16[128,16,128]{0,2,1:T(8,128)(2,1)S(1)}, u32[]{:S(2)}, u32[]{:S(2)}) async-start(bf16[128,16,128]{0,2,1:T(8,128)(2,1)} %bitcast.14), calls=%async_computation.1 | async-start | bytes 1048576 | tf_op jit(solution)/shard_map/all_to_all | solution.py:86
  119.5 18.2 %all-to-all-start.2 = ((bf16[128,16,128]{0,2,1:T(8,128)(2,1)}), bf16[128,16,128]{0,2,1:T(8,128)(2,1)S(1)}, u32[]{:S(2)}, u32[]{:S(2)}) async-start(bf16[128,16,128]{0,2,1:T(8,128)(2,1)} %bitcast.17), calls=%async_computation.2 | async-start | bytes 1048576 | tf_op jit(solution)/shard_map/all_to_all | solution.py:87
  137.8 19.1 %all-to-all-start = ((bf16[128,16,128]{0,2,1:T(8,128)(2,1)}), bf16[128,16,128]{0,2,1:T(8,128)(2,1)S(1)}, u32[]{:S(2)}, u32[]{:S(2)}) async-start(bf16[128,16,128]{0,2,1:T(8,128)(2,1)} %bitcast.10), calls=%async_computation | async-start | bytes 1048576 | tf_op jit(solution)/shard_map/all_to_all | solution.py:85
  143.5 309.6 %all-gather.11.cloned.1.call-start = ((), (), s32[]{:S(2)}) async-start(), calls=%async_computation.9 | async-start | bytes 1081344 | tf_op jit(solution)/shard_map/all_gather | solution.py:137
  157.1 17.3 %copy-start.4 = (f32[1,64,256]{2,1,0:T(8,128)S(1)}, f32[1,64,256]{2,1,0:T(8,128)}, u32[]{:S(2)}) copy-start(f32[1,64,256]{2,1,0:T(8,128)} %param.24) | copy-start | bytes 196612
  157.2 17.9 %copy-start.5 = (s32[128,8]{0,1:T(8,128)S(1)}, s32[128,8]{0,1:T(8,128)}, u32[]{:S(2)}) copy-start(s32[128,8]{0,1:T(8,128)} %param.26) | copy-start | bytes 12292
  157.2 27.2 %copy-start = (bf16[128,2048]{1,0:T(8,128)(2,1)S(1)}, bf16[128,2048]{1,0:T(8,128)(2,1)}, u32[]{:S(2)}) copy-start(bf16[128,2048]{1,0:T(8,128)(2,1)} %param.15) | copy-start | bytes 1572868
  169.5 14.6 %all-to-all-start.3 = ((bf16[16,128,128]{2,1,0:T(8,128)(2,1)}), bf16[16,128,128]{2,1,0:T(8,128)(2,1)S(1)}, u32[]{:S(2)}, u32[]{:S(2)}) async-start(bf16[16,128,128]{2,1,0:T(8,128)(2,1)} %bitcast.20), calls=%async_computation.3 | async-start | bytes 1048576 | tf_op jit(solution)/shard_map/all_to_all | solution.py:106
  174.4 419.6 %all-gather.9.cloned.1.call-start = ((), (), s32[]{:S(2)}) async-start(), calls=%async_computation.8 | async-start | bytes 1081344 | tf_op jit(solution)/shard_map/all_gather | solution.py:136
  184.4 6.4 %copy-start.9 = (f32[2048]{0:T(1024)S(1)}, f32[2048]{0:T(1024)}, u32[]{:S(2)}) copy-start(f32[2048]{0:T(1024)} %param.22) | copy-start | bytes 24580
  190.8 407.1 %copy-start.1 = (bf16[128,2048]{1,0:T(8,128)(2,1)}, bf16[128,2048]{1,0:T(8,128)(2,1)S(1)}, u32[]{:S(2)}) copy-start(bf16[128,2048]{1,0:T(8,128)(2,1)S(1)} %get-tuple-element.98) | copy-start | bytes 1572868
  190.8 6.4 copy-start.6
  192.3 119.6 %all-to-all-start.4 = ((bf16[16,16,2048]{2,1,0:T(8,128)(2,1)}), bf16[16,16,2048]{2,1,0:T(8,128)(2,1)S(1)}, u32[]{:S(2)}, u32[]{:S(2)}) async-start(bf16[16,16,2048]{2,1,0:T(8,128)(2,1)} %bitcast.24), calls=%async_computation.4 | async-start | bytes 2097152 | tf_op jit(solution)/shard_map/all_to_all | solution.py:139
  197.3 414.6 %copy-start.7 = (s32[1,17]{1,0:T(1,128)S(1)}, s32[1,17]{1,0:T(1,128)}, u32[]{:S(2)}) copy-start(s32[1,17]{1,0:T(1,128)} %param.20) | copy-start | bytes 208
  597.8 29.5 %all-to-all-start.5 = ((bf16[16,16,2048]{2,1,0:T(8,128)(2,1)}), bf16[16,16,2048]{2,1,0:T(8,128)(2,1)S(1)}, u32[]{:S(2)}, u32[]{:S(2)}) async-start(bf16[16,16,2048]{2,1,0:T(8,128)(2,1)} %convolution_convert_fusion), calls=%async_computation.5 | async-start | bytes 2097152 | tf_op jit(solution)/shard_map/all_to_all | solution.py:146
Sparse Core Ops, SparseCore 0:
  85.3 89.7 all-gather.4
  178.1 133.7 all-gather.6
  315.6 137.4 all-gather.10
  456.6 137.4 all-gather.8
where the time goes:
time: 637 us; the launch traced here: 636 us
  waiting for transfers between devices  440 us (69%)
  blocking collectives  77.1 us (12%)
  starting transfers between devices  53.2 us (8%)
  matrix products  23.4 us (4%)
  local copies, waits for them, and re-layouts  20.7 us (3%)
  between operations  14 us (2%)
  other arithmetic  7.47 us (1%)
    all_gather x1, waiting for transfers between devices, body(): lax.all_gather(up_shard.astype(jnp.bfloat16), 'dp', axis=1, tiled=True)  141 us
    all_gather x1, waiting for transfers between devices, body(): lax.all_gather(down_shard.astype(jnp.bfloat16), 'dp', axis=2, tiled=True)  139 us
    all_gather x1, waiting for transfers between devices, body(): lax.all_gather(gate_shard.astype(jnp.bfloat16), 'dp', axis=1, tiled=True)  115 us
    all_gather x1, blocking collectives, body(): columns = lax.all_gather(wo_cast, 'dp', axis=1, tiled=True)  77.1 us
    all_to_all x1, starting transfers between devices, body(): lax.all_to_all(new_keys, 'tensor', split_axis=1, concat_axis=0, tiled=True)  19.2 us
    all_to_all x1, starting transfers between devices, body(): lax.all_to_all(result, 'tensor', split_axis=0, concat_axis=0, tiled=True)  14 us
  transfers between devices with their start and end apart: 10, of which 8 were waited for; matrix products, arithmetic and copies ran while one was open for 7% of the time, Pallas kernels for 0%

commit v1 on v0

--- a/solution.py
+++ b/solution.py
@@ -132,7 +132,15 @@
     ).astype(jnp.bfloat16)
     outgoing = jnp.repeat(outgoing, SPLIT, axis=0)
     gate_full, up_full, down_full = (
-        lax.all_gather(gate_shard.astype(jnp.bfloat16), "dp", axis=1, tiled=True),
+        jnp.concatenate(
+            lax.all_to_all(
+                jnp.stack([gate_shard.astype(jnp.bfloat16)] * lax.axis_size("dp")),
+                axis_name="dp",
+                split_axis=0,
+                concat_axis=0,
+            ),
+            axis=1,
+        ),
         lax.all_gather(up_shard.astype(jnp.bfloat16), "dp", axis=1, tiled=True),
         lax.all_gather(down_shard.astype(jnp.bfloat16), "dp", axis=2, tiled=True),
     )

time: 637 us -> 517 us (0.81)
  waiting for transfers between devices: 440 us -> 316 us
    all_gather x1 -> x0, waiting for transfers between devices: 115 us -> none  [body(): lax.all_gather(gate_shard.astype(jnp.bfloat16), 'dp', axis=1, tiled=True)]
    all_gather x1, waiting for transfers between devices: 141 us -> 67.5 us  [body(): lax.all_gather(up_shard.astype(jnp.bfloat16), 'dp', axis=1, tiled=True)]
    all_to_all x0 -> x1, waiting for transfers between devices: none -> 43.5 us  [body(): lax.all_to_all(jnp.stack([gate_shard.astype(jnp.bfloat16)] * lax.axis_siz...]
    all_to_all x1, waiting for transfers between devices: 0.01 us -> 15.2 us  [body(): lax.all_to_all(outgoing, 'tensor', split_axis=0, concat_axis=0, tiled=True)]
  transfers between devices with their start and end apart: 10 -> 10, of which waited for: 8 -> 9; matrix products, arithmetic and copies ran while one was open for 7% -> 8% of each run, Pallas kernels for 0% -> 0%
where the time goes in v1:
time: 517 us; the launch traced here: 516 us
  waiting for transfers between devices  316 us (61%)
  blocking collectives  77.1 us (15%)
  starting transfers between devices  58 us (11%)
  local copies, waits for them, and re-layouts  22.9 us (4%)
  matrix products  22.3 us (4%)
  between operations  14 us (3%)
  other arithmetic  6.03 us (1%)
    all_gather x1, waiting for transfers between devices, body(): lax.all_gather(down_shard.astype(jnp.bfloat16), 'dp', axis=2, tiled=True)  141 us
    all_gather x1, blocking collectives, body(): columns = lax.all_gather(wo_cast, 'dp', axis=1, tiled=True)  77.1 us
    all_gather x1, waiting for transfers between devices, body(): lax.all_gather(up_shard.astype(jnp.bfloat16), 'dp', axis=1, tiled=True)  67.5 us
    all_to_all x1, waiting for transfers between devices, body(): lax.all_to_all(jnp.stack([gate_shard.astype(jnp.bfloat16)] * lax.axis_siz...  43.5 us
    all_to_all x1, starting transfers between devices, body(): lax.all_to_all(new_keys, 'tensor', split_axis=1, concat_axis=0, tiled=True)  19.2 us
    all_to_all x1, waiting for transfers between devices, body(): lax.all_to_all(outgoing, 'tensor', split_axis=0, concat_axis=0, tiled=True)  15.2 us
    all_to_all x1, starting transfers between devices, body(): lax.all_to_all(result, 'tensor', split_axis=0, concat_axis=0, tiled=True)  14 us
    all_to_all x1, waiting for transfers between devices, body(): lax.all_to_all(queries, 'tensor', split_axis=1, concat_axis=0, tiled=True)  13 us
  transfers between devices with their start and end apart: 10, of which 9 were waited for; matrix products, arithmetic and copies ran while one was open for 8% of the time, Pallas kernels for 0%

profile of v1, /device:TPU:1, one launch (start us, length us, event | category | flops | bytes accessed | tf_op | source)
XLA Modules:
  0.0 516.0 jit_solution(8717750398816490362)
XLA Ops:
  8.0 77.1 %all_gather.12 = bf16[128,2048]{0,1:T(8,128)(2,1)} all-gather(bf16[128,64]{0,1:T(8,128)(2,1)S(1)} %convert_element_type.70), channel_id=1, replica_groups=mesh['dp'=32,'tensor'=16] {'dp'}, dimensions={1}, use_global_device_ids=true | all-gather | bytes 540672 | tf_op jit(solution)/shard_map/all_gather | solution.py:108
  85.1 2.0 copy.76
  87.2 19.2 %all-to-all-start.1 = ((bf16[128,16,128]{0,2,1:T(8,128)(2,1)}), bf16[128,16,128]{0,2,1:T(8,128)(2,1)S(1)}, u32[]{:S(2)}, u32[]{:S(2)}) async-start(bf16[128,16,128]{0,2,1:T(8,128)(2,1)} %bitcast.14), calls=%async_computation.1 | async-start | bytes 1048576 | tf_op jit(solution)/shard_map/all_to_all | solution.py:86
  106.3 2.0 copy.78
  108.4 11.2 %all-to-all-done.1 = bf16[128,16,128]{0,2,1:T(8,128)(2,1)S(1)} async-done(((bf16[128,16,128]{0,2,1:T(8,128)(2,1)}), bf16[128,16,128]{0,2,1:T(8,128)(2,1)S(1)}, u32[]{:S(2)}, u32[]{:S(2)}) %all-to-all-start.1) | async-done | bytes 524320 | tf_op jit(solution)/shard_map/all_to_all | solution.py:86
  119.6 4.2 all-to-all-start.2
  123.8 1.0 copy.74
  124.8 12.5 %all-to-all-done.2 = bf16[128,16,128]{0,2,1:T(8,128)(2,1)S(1)} async-done(((bf16[128,16,128]{0,2,1:T(8,128)(2,1)}), bf16[128,16,128]{0,2,1:T(8,128)(2,1)S(1)}, u32[]{:S(2)}, u32[]{:S(2)}) %all-to-all-start.2) | async-done | bytes 524320 | tf_op jit(solution)/shard_map/all_to_all | solution.py:87
  137.3 4.8 all-to-all-start
  143.0 13.0 %all-to-all-done = bf16[128,16,128]{0,2,1:T(8,128)(2,1)S(1)} async-done(((bf16[128,16,128]{0,2,1:T(8,128)(2,1)}), bf16[128,16,128]{0,2,1:T(8,128)(2,1)S(1)}, u32[]{:S(2)}, u32[]{:S(2)}) %all-to-all-start) | async-done | bytes 524320 | tf_op jit(solution)/shard_map/all_to_all | solution.py:85
  156.3 12.3 %while.10 = (s32[]{:T(128)}, bf16[4,512,128]{2,1,0:T(8,128)(2,1)}, s32[4,512]{1,0:T(4,128)S(1)}, s32[2048]{0:T(1024)S(1)}, bf16[4,512,1,128]{3,1,2,0:T(8,128)(2,...) while((s32[]{:T(128)}, bf16[4,512,128]{2,1,0:T(8,128)(2,1)}, ...), condition=%wide.region_5.6_spmd, body=%wide.region_2.0_spmd.sunk | while | flops 545389568 | bytes 13918813 | solution.py:64
  157.9 1.5 fusion.85
  161.0 1.5 fusion.85
  164.1 1.5 fusion.85
  167.1 1.4 fusion.85
  169.4 5.4 %all-to-all-start.3 = ((bf16[16,128,128]{2,1,0:T(8,128)(2,1)}), bf16[16,128,128]{2,1,0:T(8,128)(2,1)S(1)}, u32[]{:S(2)}, u32[]{:S(2)}) async-start(bf16[16,128,128]{2,1,0:T(8,128)(2,1)} %bitcast.20), calls=%async_computation.3 | async-start | bytes 1048576 | tf_op jit(solution)/shard_map/all_to_all | solution.py:106
  174.8 9.7 %all-to-all-done.3 = bf16[16,128,128]{2,1,0:T(8,128)(2,1)S(1)} async-done(((bf16[16,128,128]{2,1,0:T(8,128)(2,1)}), bf16[16,128,128]{2,1,0:T(8,128)(2,1)S(1)}, u32[]{:S(2)}, u32[]{:S(2)}) %all-to-all-start.3) | async-done | bytes 524320 | tf_op jit(solution)/shard_map/all_to_all | solution.py:106
  184.5 1.1 stack.2
  185.6 4.1 all-to-all-start.5
  192.0 6.4 %fusion.28 = (f32[128]{0:T(128)S(1)}, bf16[128,2048]{1,0:T(8,128)(2,1)S(1)}) fusion(bf16[128,2048]{0,1:T(8,128)(2,1)S(1)} %bitcast.111, bf16[2048,2048]{0,1:T(8,128)(2,1)} %all-gather.4.cloned.1.call-done, bf16[128,2048]{1,0:T(8,128)(2,1)S(1)} %copy-done), kind=kOutput, calls=%fused_computation.30 | convolution fusion | flops 1075314560 | bytes 9961984 | tf_op jit(solution)/shard_map/dot_general | solution.py:109
  198.8 43.5 %all-to-all-done.5 = bf16[32,1,64,256]{3,2,1,0:T(8,128)(2,1)S(1)} async-done(((bf16[32,1,64,256]{3,2,1,0:T(8,128)(2,1)}), bf16[32,1,64,256]{3,2,1,0:T(8,128)(2,1)S(1)}, u32[]{:S(2)}, u32[]{:S(2)}) %all-to-all-start.5) | async-done | bytes 1048608 | tf_op jit(solution)/shard_map/all_to_all | solution.py:136
  242.3 1.1 broadcast_in_dim.27
  243.4 6.1 %all-to-all-start.4 = ((bf16[16,16,2048]{2,1,0:T(8,128)(2,1)}), bf16[16,16,2048]{2,1,0:T(8,128)(2,1)S(1)}, u32[]{:S(2)}, u32[]{:S(2)}) async-start(bf16[16,16,2048]{2,1,0:T(8,128)(2,1)} %bitcast.24), calls=%async_computation.4 | async-start | bytes 2097152 | tf_op jit(solution)/shard_map/all_to_all | solution.py:147
  249.8 15.2 %all-to-all-done.4 = bf16[16,16,2048]{2,1,0:T(8,128)(2,1)S(1)} async-done(((bf16[16,16,2048]{2,1,0:T(8,128)(2,1)}), bf16[16,16,2048]{2,1,0:T(8,128)(2,1)S(1)}, u32[]{:S(2)}, u32[]{:S(2)}) %all-to-all-start.4) | async-done | bytes 1048608 | tf_op jit(solution)/shard_map/all_to_all | solution.py:147
  265.5 67.5 %all-gather.6.cloned.1.call-done = bf16[1,2048,256]{2,1,0:T(8,128)(2,1)} async-done(((bf16[1,64,256]{2,1,0:T(8,128)(2,1)}), bf16[1,2048,256]{2,1,0:T(8,128)(2,1)}) %all-gather.6.cloned.1.call-update) | async-done | bytes 1048592 | tf_op jit(solution)/shard_map/all_gather | solution.py:144
  333.1 141.1 %all-gather.8.cloned.1.call-done = bf16[1,256,2048]{1,2,0:T(8,128)(2,1)} async-done(((bf16[1,256,64]{1,2,0:T(8,128)(2,1)}), bf16[1,256,2048]{1,2,0:T(8,128)(2,1)}) %all-gather.8.cloned.1.call-update) | async-done | bytes 1048592 | tf_op jit(solution)/shard_map/all_gather | solution.py:145
  474.2 3.8 convolution_convert_fusion
  478.0 14.0 %all-to-all-start.6 = ((bf16[16,16,2048]{2,1,0:T(8,128)(2,1)}), bf16[16,16,2048]{2,1,0:T(8,128)(2,1)S(1)}, u32[]{:S(2)}, u32[]{:S(2)}) async-start(bf16[16,16,2048]{2,1,0:T(8,128)(2,1)} %convolution_convert_fusion), calls=%async_computation.6 | async-start | bytes 2097152 | tf_op jit(solution)/shard_map/all_to_all | solution.py:154
  492.3 6.9 %scatter_custom_fusion = bf16[2176,128]{1,0:T(8,128)(2,1)} fusion(s32[2048]{0:T(1024)S(1)} %bitcast.124, bf16[2048,128]{1,0:T(8,128)(2,1)} %bitcast.119, bf16[]{:T(256)} %constant.81.clone.1), kind=kCustom, calls=%fused_computation.40 | custom fusion | bytes 557568 | tf_op jit(solution)/shard_map/scatter | solution.py:96
  499.1 6.5 %scatter_custom_fusion.1 = bf16[2176,128]{1,0:T(8,128)(2,1)} fusion(s32[2048]{0:T(1024)S(1)} %bitcast.125, bf16[2048,128]{1,0:T(8,128)(2,1)S(1)} %bitcast.109, bf16[]{:T(256)} %constant.81.clone.1), kind=kCustom, calls=%fused_computation.38 | custom fusion | bytes 557058 | tf_op jit(solution)/shard_map/scatter | solution.py:102
  505.7 1.8 all-to-all-done.6
  507.7 1.8 fusion.26
  (74 shorter events, 12.9 us)
Async XLA Ops:
  7.2 116.6 %copy-start.2 = (bf16[128,2048]{1,0:T(8,128)(2,1)S(1)}, bf16[128,2048]{1,0:T(8,128)(2,1)}, u32[]{:S(2)}) copy-start(bf16[128,2048]{1,0:T(8,128)(2,1)} %param.16) | copy-start | bytes 1572868
  7.2 134.9 %copy-start.10 = (s32[1,2]{1,0:T(1,128)S(1)}, s32[1,2]{1,0:T(1,128)}, u32[]{:S(2)}) copy-start(s32[1,2]{1,0:T(1,128)} %param.19) | copy-start | bytes 28
  7.2 184.8 %all-gather.4.cloned.1.call-start = ((), (), s32[]{:S(2)}) async-start(), calls=%async_computation.7 | async-start | bytes 8912896 | tf_op jit(solution)/shard_map/all_gather | solution.py:111
  87.2 32.4 %all-to-all-start.1 = ((bf16[128,16,128]{0,2,1:T(8,128)(2,1)}), bf16[128,16,128]{0,2,1:T(8,128)(2,1)S(1)}, u32[]{:S(2)}, u32[]{:S(2)}) async-start(bf16[128,16,128]{0,2,1:T(8,128)(2,1)} %bitcast.14), calls=%async_computation.1 | async-start | bytes 1048576 | tf_op jit(solution)/shard_map/all_to_all | solution.py:86
  119.6 17.7 %all-to-all-start.2 = ((bf16[128,16,128]{0,2,1:T(8,128)(2,1)}), bf16[128,16,128]{0,2,1:T(8,128)(2,1)S(1)}, u32[]{:S(2)}, u32[]{:S(2)}) async-start(bf16[128,16,128]{0,2,1:T(8,128)(2,1)} %bitcast.17), calls=%async_computation.2 | async-start | bytes 1048576 | tf_op jit(solution)/shard_map/all_to_all | solution.py:87
  137.3 18.7 %all-to-all-start = ((bf16[128,16,128]{0,2,1:T(8,128)(2,1)}), bf16[128,16,128]{0,2,1:T(8,128)(2,1)S(1)}, u32[]{:S(2)}, u32[]{:S(2)}) async-start(bf16[128,16,128]{0,2,1:T(8,128)(2,1)} %bitcast.10), calls=%async_computation | async-start | bytes 1048576 | tf_op jit(solution)/shard_map/all_to_all | solution.py:85
  156.3 18.5 %copy-start.4 = (f32[1,64,256]{2,1,0:T(8,128)S(1)}, f32[1,64,256]{2,1,0:T(8,128)}, u32[]{:S(2)}) copy-start(f32[1,64,256]{2,1,0:T(8,128)} %param.23) | copy-start | bytes 196612
  168.6 0.8 copy-start.3
  168.6 21.2 %copy-start.5 = (f32[1,64,256]{2,1,0:T(8,128)S(1)}, f32[1,64,256]{2,1,0:T(8,128)}, u32[]{:S(2)}) copy-start(f32[1,64,256]{2,1,0:T(8,128)} %param.24) | copy-start | bytes 196612
  168.6 21.9 %copy-start.6 = (f32[1,256,64]{1,2,0:T(8,128)S(1)}, f32[1,256,64]{1,2,0:T(8,128)}, u32[]{:S(2)}) copy-start(f32[1,256,64]{1,2,0:T(8,128)} %param.25) | copy-start | bytes 196612
  168.6 22.6 %copy-start.7 = (s32[128,8]{0,1:T(8,128)S(1)}, s32[128,8]{0,1:T(8,128)}, u32[]{:S(2)}) copy-start(s32[128,8]{0,1:T(8,128)} %param.26) | copy-start | bytes 12292
  168.6 23.4 %copy-start = (bf16[128,2048]{1,0:T(8,128)(2,1)S(1)}, bf16[128,2048]{1,0:T(8,128)(2,1)}, u32[]{:S(2)}) copy-start(bf16[128,2048]{1,0:T(8,128)(2,1)} %param.15) | copy-start | bytes 1572868
  169.4 15.1 %all-to-all-start.3 = ((bf16[16,128,128]{2,1,0:T(8,128)(2,1)}), bf16[16,128,128]{2,1,0:T(8,128)(2,1)S(1)}, u32[]{:S(2)}, u32[]{:S(2)}) async-start(bf16[16,128,128]{2,1,0:T(8,128)(2,1)} %bitcast.20), calls=%async_computation.3 | async-start | bytes 1048576 | tf_op jit(solution)/shard_map/all_to_all | solution.py:106
  185.6 56.7 %all-to-all-start.5 = ((bf16[32,1,64,256]{3,2,1,0:T(8,128)(2,1)}), bf16[32,1,64,256]{3,2,1,0:T(8,128)(2,1)S(1)}, u32[]{:S(2)}, u32[]{:S(2)}) async-start(bf16[32,1,64,256]{3,2,1,0:T(8,128)(2,1)} %stack.2), calls=%async_computation.5 | async-start | bytes 2097152 | tf_op jit(solution)/shard_map/all_to_all | solution.py:136
  189.7 143.3 %all-gather.6.cloned.1.call-start = ((), (), s32[]{:S(2)}) async-start(), calls=%async_computation.8 | async-start | bytes 1081344 | tf_op jit(solution)/shard_map/all_gather | solution.py:144
  190.5 283.7 %all-gather.8.cloned.1.call-start = ((), (), s32[]{:S(2)}) async-start(), calls=%async_computation.9 | async-start | bytes 1081344 | tf_op jit(solution)/shard_map/all_gather | solution.py:145
  192.0 6.5 %copy-start.11 = (f32[2048]{0:T(1024)S(1)}, f32[2048]{0:T(1024)}, u32[]{:S(2)}) copy-start(f32[2048]{0:T(1024)} %param.22) | copy-start | bytes 24580
  198.4 45.0 %copy-start.1 = (bf16[128,2048]{1,0:T(8,128)(2,1)}, bf16[128,2048]{1,0:T(8,128)(2,1)S(1)}, u32[]{:S(2)}) copy-start(bf16[128,2048]{1,0:T(8,128)(2,1)S(1)} %get-tuple-element.98) | copy-start | bytes 1572868
  198.4 51.3 %copy-start.8 = (f32[128,8]{0,1:T(8,128)S(1)}, f32[128,8]{0,1:T(8,128)}, u32[]{:S(2)}) copy-start(f32[128,8]{0,1:T(8,128)} %param.27) | copy-start | bytes 12292
  243.4 21.7 %all-to-all-start.4 = ((bf16[16,16,2048]{2,1,0:T(8,128)(2,1)}), bf16[16,16,2048]{2,1,0:T(8,128)(2,1)S(1)}, u32[]{:S(2)}, u32[]{:S(2)}) async-start(bf16[16,16,2048]{2,1,0:T(8,128)(2,1)} %bitcast.24), calls=%async_computation.4 | async-start | bytes 2097152 | tf_op jit(solution)/shard_map/all_to_all | solution.py:147
  265.1 227.0 %copy-start.9 = (s32[1,17]{1,0:T(1,128)S(1)}, s32[1,17]{1,0:T(1,128)}, u32[]{:S(2)}) copy-start(s32[1,17]{1,0:T(1,128)} %param.20) | copy-start | bytes 208
  478.0 29.5 %all-to-all-start.6 = ((bf16[16,16,2048]{2,1,0:T(8,128)(2,1)}), bf16[16,16,2048]{2,1,0:T(8,128)(2,1)S(1)}, u32[]{:S(2)}, u32[]{:S(2)}) async-start(bf16[16,16,2048]{2,1,0:T(8,128)(2,1)} %convolution_convert_fusion), calls=%async_computation.6 | async-start | bytes 2097152 | tf_op jit(solution)/shard_map/all_to_all | solution.py:154
Sparse Core Ops, SparseCore 0:
  85.3 88.2 all-gather.3
  194.2 138.7 all-gather.5
  336.8 137.4 all-gather.7
